TPU v7x, 256 devices: a whole 4x4x8 slice. The times are simulated.
256 devices in a mesh: gx: 16 (over z, core), gy: 16 (over y, x).
Axes of the slice: x: 4, y: 4, z: 8, core: 2. Of those that a mesh axis runs over, the one named last changes fastest.
Arguments:
- right_side: float32 [256, 128, 1024], P('gx', 'gy'), may hold values from -340 to 340
- start_guess: float32 [256, 128, 1024], P('gx', 'gy'), may hold values from -1.8 to 1.8
- couple_x: float32 [256, 128, 64], P('gx', 'gy'), may hold values from 0.3 to 3
- couple_y: float32 [256, 128, 64], P('gx', 'gy'), may hold values from 0.3 to 3
- couple_z: float32 [256, 128, 64], P('gx', 'gy'), may hold values from 0.3 to 3
- reaction: float32 [256, 128, 64], P('gx', 'gy'), may hold values from 0.01 to 0.1
Outputs:
- solution: float32 [256, 128, 1024], P('gx', 'gy')
- residual: float32 [256, 128, 1024], P('gx', 'gy')
All inputs are finite; a program needn't handle non-finite values.
Results may differ from a plain program's by a relative error of at most 0.0003.
Values sent between devices are 32-bit elements; how exact they have to be, the bound alone decides.
No kernel may reach another device: no remote copies, remote signals or barrier semaphores. Data moves between devices by JAX's collectives and lax.ppermute only.
A program may use at most 64 MiB of HBM per device.

v0:
```python
import jax
import jax.numpy as jnp
from jax import lax
from jax.sharding import PartitionSpec as P

ITERS = 2
SWEEPS = 4
FACT_SWEEPS = 3
HIGH = lax.Precision.HIGHEST


def passed_along(block, axis, distance):
    devices = range(lax.axis_size(axis))
    route = [(i - distance, i) for i in devices if i - distance in devices]
    return lax.ppermute(block, axis, route)


def padded_2(block, sides, width):
    for axis, dim in sides:
        count = lax.axis_size(axis)
        forward = [(i, i + 1) for i in range(count - 1)]
        backward = [(target, source) for source, target in forward]
        low = lax.ppermute(
            lax.slice_in_dim(block, block.shape[dim] - width, None, axis=dim), axis, forward
        )
        high = lax.ppermute(lax.slice_in_dim(block, 0, width, axis=dim), axis, backward)
        block = jnp.concatenate([low, block, high], axis=dim)
    return block


def low_shift(values, along):
    count = values.shape[along]
    blank = jnp.zeros_like(lax.slice_in_dim(values, 0, 1, axis=along))
    return jnp.concatenate([blank, lax.slice_in_dim(values, 0, count - 1, axis=along)], axis=along)


def up_shift(values, along):
    count = values.shape[along]
    blank = jnp.zeros_like(lax.slice_in_dim(values, 0, 1, axis=along))
    return jnp.concatenate([lax.slice_in_dim(values, 1, count, axis=along), blank], axis=along)


def block_gram(former, latter, count_rhs):
    cells = former.shape[0] * former.shape[1]
    left = former.reshape(cells, count_rhs, -1)
    right = latter.reshape(cells, count_rhs, -1)
    return jnp.einsum("psz,ptz->st", left, right, precision=HIGH)


def mix_block(values, matrix):
    rows_x, rows_y, flat_len = values.shape
    count_rhs = matrix.shape[0]
    split = values.reshape(rows_x * rows_y, count_rhs, flat_len // count_rhs)
    return jnp.einsum("psz,st->ptz", split, matrix, precision=HIGH).reshape(
        rows_x, rows_y, flat_len
    )


def chol_factor(gram_mat):
    low_factor = jnp.linalg.cholesky(gram_mat)
    eye_mat = jnp.eye(gram_mat.shape[0], dtype=gram_mat.dtype)
    inverse = lax.linalg.triangular_solve(low_factor, eye_mat, left_side=True, lower=True)
    return (low_factor.T, inverse.T)


def solve_small(columns, first_factor):
    hessen = jnp.concatenate(columns, axis=1)
    count_rhs = first_factor.shape[0]
    target = jnp.dot(hessen[:count_rhs].T, first_factor, precision=HIGH)
    normal = jnp.dot(hessen.T, hessen, precision=HIGH)
    low_factor = jnp.linalg.cholesky(normal)
    partial_sol = lax.linalg.triangular_solve(low_factor, target, left_side=True, lower=True)
    return lax.linalg.triangular_solve(
        low_factor, partial_sol, left_side=True, lower=True, transpose_a=True
    )


def body(right_side, start_guess, couple_x, couple_y, couple_z, reaction):
    rows_x, rows_y, flat_len = right_side.shape
    layers = couple_z.shape[2]
    count_rhs = flat_len // layers
    depth = jnp.arange(flat_len, dtype=jnp.int32) % layers
    keep_first = (depth != 0).astype(jnp.float32)
    keep_last = (depth != layers - 1).astype(jnp.float32)

    def low_z(values):
        return low_shift(values, 2) * keep_first

    def up_z(values):
        return up_shift(values, 2) * keep_last

    def tiled(values):
        return jnp.tile(values, (1, 1, count_rhs))

    edge_x = passed_along(couple_x[-1:], "gx", 1)
    edge_y = passed_along(couple_y[:, -1:], "gy", 1)
    after_x = tiled(couple_x)
    after_y = tiled(couple_y)
    after_z = tiled(couple_z)
    before_x = tiled(jnp.concatenate([edge_x, couple_x[:-1]], axis=0))
    before_y = tiled(jnp.concatenate([edge_y, couple_y[:, :-1]], axis=1))
    before_z = low_z(after_z)
    diagonal = tiled(reaction) + after_x + before_x + after_y + before_y + after_z + before_z

    def apply_op(values):
        padded = padded_2(values, (("gx", 0), ("gy", 1)), 1)
        centre = padded[1:-1, 1:-1]
        return (
            diagonal * centre
            - after_x * padded[2:, 1:-1]
            - before_x * padded[:-2, 1:-1]
            - after_y * padded[1:-1, 2:]
            - before_y * padded[1:-1, :-2]
            - after_z * up_z(centre)
            - before_z * low_z(centre)
        )

    lows = (low_shift(after_x, 0), low_shift(after_y, 1), before_z)
    ups = (
        up_shift(jnp.ones_like(after_x), 0) * after_x,
        up_shift(jnp.ones_like(after_y), 1) * after_y,
        after_z,
    )
    pivots = diagonal
    for repeat in range(FACT_SWEEPS):
        inv_now = 1.0 / pivots
        pivots = (
            diagonal
            - lows[0] * lows[0] * low_shift(inv_now, 0)
            - lows[1] * lows[1] * low_shift(inv_now, 1)
            - lows[2] * lows[2] * low_z(inv_now)
        )
    inv_piv = 1.0 / pivots

    def total_gram(former, latter):
        return lax.psum(block_gram(former, latter, count_rhs), ("gx", "gy"))

    start_res = right_side - apply_op(start_guess)
    first_factor, first_inv = chol_factor(total_gram(start_res, start_res))
    basis_set = [mix_block(start_res, first_inv)]
    precond_set = []
    image_set = []
    columns = []
    for column in range(ITERS):
        source = basis_set[column]
        lower_sol = inv_piv * source
        for precondition_repeat in range(SWEEPS):
            lower_sol = inv_piv * (
                source
                + lows[0] * low_shift(lower_sol, 0)
                + lows[1] * low_shift(lower_sol, 1)
                + lows[2] * low_z(lower_sol)
            )
        upper_sol = lower_sol
        for precondition_repeat in range(SWEEPS):
            upper_sol = lower_sol + inv_piv * (
                ups[0] * up_shift(upper_sol, 0)
                + ups[1] * up_shift(upper_sol, 1)
                + ups[2] * up_z(upper_sol)
            )
        image = apply_op(upper_sol)
        precond_set.append(upper_sol)
        image_set.append(image)
        local_proj = jnp.stack([block_gram(member, image, count_rhs) for member in basis_set])
        stacked = lax.psum(local_proj, ("gx", "gy"))
        projections = [stacked[member] for member in range(len(basis_set))]
        removed = mix_block(basis_set[0], projections[0])
        for member in range(1, len(basis_set)):
            removed = removed + mix_block(basis_set[member], projections[member])
        perp = image - removed
        next_factor, next_inv = chol_factor(total_gram(perp, perp))
        if column + 1 < ITERS:
            basis_set.append(mix_block(perp, next_inv))
        blank = jnp.zeros(((ITERS - 1 - column) * count_rhs, count_rhs), dtype=next_factor.dtype)
        columns.append(jnp.concatenate(projections + [next_factor, blank], axis=0))
    coeffs = solve_small(columns, first_factor)
    solution = start_guess
    for column in range(ITERS):
        solution = solution + mix_block(
            precond_set[column], coeffs[column * count_rhs : (column + 1) * count_rhs]
        )
    residual = right_side - apply_op(solution)
    return (solution, residual)


def solution(mesh):
    return jax.shard_map(
        body,
        mesh=mesh,
        in_specs=(
            P("gx", "gy", None),
            P("gx", "gy", None),
            P("gx", "gy", None),
            P("gx", "gy", None),
            P("gx", "gy", None),
            P("gx", "gy", None),
        ),
        out_specs=(P("gx", "gy", None), P("gx", "gy", None)),
        check_vma=False,
    )
```

profile of v0, /device:TPU:40, one launch (start us, length us, event | category | flops | bytes accessed | tf_op | source)
XLA Modules:
  0.0 608.5 jit_solution(9430777300080090725)
XLA Ops:
  3.4 3.6 collective-permute-start.2
  9.3 3.4 collective-permute-start.1
  29.7 4.6 collective-permute-start.4
  39.6 3.6 collective-permute-done.5
  43.2 3.8 fusion.36
  49.3 3.1 convolution_bitcast_fusion.12
  52.4 2.5 copy.35
  57.6 77.3 %psum.35 = f32[16,16]{0,1:T(8,128)S(1)} all-reduce(f32[16,16]{0,1:T(8,128)S(1)} %convolution_bitcast_fusion.12), channel_id=1, replica_groups=mesh['gx'=16,'gy'=16] {'gx','gy'}, use_global_device_ids=true, to_apply=%region_0.1 | all-reduce | flops 256 | bytes 2048 | tf_op jit(solution)/shard_map/psum | solution.py:136
  153.0 2.8 collective-permute-start.6
  157.7 3.3 collective-permute-done.7
  161.1 4.6 collective-permute-start.8
  168.1 6.2 %collective-permute-done.9 = f32[18,1,1024]{2,1,0:T(1,128)S(1)} collective-permute-done((f32[18,1,1024]{2,1,0:T(1,128)S(1)}, f32[18,1,1024]{2,1,0:T(1,128)S(1)}, u32[]{:S(2)}, u32[]{:S(2)}) %collective-permute-start.9) | collective-permute-done | bytes 73760 | tf_op jit(solution)/shard_map/ppermute | solution.py:23
  178.0 2.5 copy.37
  182.5 71.4 %psum.36 = f32[16,16]{0,1:T(8,128)S(1)} all-reduce(f32[16,16]{0,1:T(8,128)S(1)} %convolution_bitcast_fusion.10), channel_id=1, replica_groups=mesh['gx'=16,'gy'=16] {'gx','gy'}, use_global_device_ids=true, to_apply=%region_3.6 | all-reduce | flops 256 | bytes 2048 | tf_op jit(solution)/shard_map/psum | solution.py:165
  256.3 2.5 copy.39
  265.4 2.5 copy.44
  268.0 3.1 convolution_bitcast_fusion.9
  271.0 74.0 %psum.37 = f32[16,16]{0,1:T(8,128)S(1)} all-reduce(f32[16,16]{0,1:T(8,128)S(1)} %convolution_bitcast_fusion.9), channel_id=1, replica_groups=mesh['gx'=16,'gy'=16] {'gx','gy'}, use_global_device_ids=true, to_apply=%region_4.7 | all-reduce | flops 256 | bytes 2048 | tf_op jit(solution)/shard_map/psum | solution.py:136
  351.8 2.5 copy.45
  364.9 2.9 collective-permute-start.10
  372.3 2.6 copy.56
  375.0 4.6 collective-permute-start.12
  384.0 2.5 copy.58
  388.1 2.9 fusion.15
  393.3 2.6 copy.46
  398.7 75.0 %psum.38 = f32[2,16,16]{1,2,0:T(8,128)S(1)} all-reduce(f32[2,16,16]{1,2,0:T(8,128)S(1)} %pad_maximum_fusion.39), channel_id=1, replica_groups=mesh['gx'=16,'gy'=16] {'gx','gy'}, use_global_device_ids=true, to_apply=%region_5.8 | all-reduce | flops 512 | bytes 4096 | tf_op jit(solution)/shard_map/psum | solution.py:165
  483.3 3.1 convolution_bitcast_fusion.5
  486.5 74.9 %psum.39 = f32[16,16]{0,1:T(8,128)S(1)} all-reduce(f32[16,16]{0,1:T(8,128)S(1)} %convolution_bitcast_fusion.5), channel_id=1, replica_groups=mesh['gx'=16,'gy'=16] {'gx','gy'}, use_global_device_ids=true, to_apply=%region_6.9 | all-reduce | flops 256 | bytes 2048 | tf_op jit(solution)/shard_map/psum | solution.py:136
  565.4 2.9 cholesky.41
  590.7 2.8 collective-permute-done.15
  593.6 4.7 collective-permute-start.16
  600.6 6.2 %collective-permute-done.17 = f32[18,1,1024]{2,1,0:T(1,128)S(1)} collective-permute-done((f32[18,1,1024]{2,1,0:T(1,128)S(1)}, f32[18,1,1024]{2,1,0:T(1,128)S(1)}, u32[]{:S(2)}, u32[]{:S(2)}) %collective-permute-start.17) | collective-permute-done | bytes 73760 | tf_op jit(solution)/shard_map/ppermute | solution.py:23
  (240 shorter events, 141.7 us)
Async XLA Ops:
  0.6 6.4 %copy-start.24 = (f32[16,8,64]{2,1,0:T(8,128)S(1)}, f32[16,8,64]{2,1,0:T(8,128)}, u32[]{:S(2)}) copy-start(f32[16,8,64]{2,1,0:T(8,128)} %param.11) | copy-start | bytes 98308
  0.6 8.6 %copy-start.23 = (f32[16,8,64]{2,1,0:T(8,128)S(1)}, f32[16,8,64]{2,1,0:T(8,128)}, u32[]{:S(2)}) copy-start(f32[16,8,64]{2,1,0:T(8,128)} %param.12) | copy-start | bytes 98308
  1.5 27.3 %collective-permute-start.3 = (f32[1,8,1024]{2,1,0:T(8,128)S(1)}, f32[1,8,1024]{2,1,0:T(8,128)S(1)}, u32[]{:S(2)}, u32[]{:S(2)}) collective-permute-start(f32[1,8,1024]{2,1,0:T(8,128)S(1)} %get-tuple-element.31), channel_id=1, source_target_pairs={{0,16},{16,32},{32,48},{48,64},{64,80},{80,96},{96,112},{112,128},... | collective-permute-start | bytes 98312 | tf_op jit(solution)/shard_map/ppermute | solution.py:23
  3.4 25.4 %collective-permute-start.2 = (f32[1,8,1024]{2,1,0:T(8,128)S(1)}, f32[1,8,1024]{2,1,0:T(8,128)S(1)}, u32[]{:S(2)}, u32[]{:S(2)}) collective-permute-start(f32[1,8,1024]{2,1,0:T(8,128)S(1)} %get-tuple-element.30), channel_id=1, source_target_pairs={{16,0},{32,16},{48,32},{64,48},{80,64},{96,80},{112,96},{128,112},... | collective-permute-start | bytes 98312 | tf_op jit(solution)/shard_map/ppermute | solution.py:26
  7.1 18.2 %collective-permute-start = (f32[1,8,64]{2,1,0:T(8,128)S(1)}, f32[1,8,64]{2,1,0:T(8,128)S(1)}, u32[]{:S(2)}, u32[]{:S(2)}) collective-permute-start(f32[1,8,64]{2,1,0:T(8,128)S(1)} %slice.369), channel_id=1, source_target_pairs={{0,16},{16,32},{32,48},{48,64},{64,80},{80,96},{96,112},{112,128},... | collective-permute-start | bytes 6152 | tf_op jit(solution)/shard_map/ppermute | solution.py:15
  9.3 26.9 %collective-permute-start.1 = (f32[16,1,64]{2,1,0:T(1,128)S(1)}, f32[16,1,64]{2,1,0:T(1,128)S(1)}, u32[]{:S(2)}, u32[]{:S(2)}) collective-permute-start(f32[16,1,64]{2,1,0:T(1,128)S(1)} %slice.371), channel_id=1, source_target_pairs={{0,1},{1,2},{2,3},{3,4},{4,5},{5,6},{6,7},{7,8},{8,9},{9,10},{10,1... | collective-permute-start | bytes 12296 | tf_op jit(solution)/shard_map/ppermute | solution.py:15
  26.3 2.4 copy-start.7
  29.7 9.9 %collective-permute-start.4 = (f32[18,1,1024]{2,1,0:T(1,128)S(1)}, f32[18,1,1024]{2,1,0:T(1,128)S(1)}, u32[]{:S(2)}, u32[]{:S(2)}) collective-permute-start(f32[18,1,1024]{2,1,0:T(1,128)S(1)} %get-tuple-element.14), channel_id=1, source_target_pairs={{1,0},{2,1},{3,2},{4,3},{5,4},{6,5},{7,6},{8,7},{9,8},{10,9},{11,1... | collective-permute-start | bytes 221192 | tf_op jit(solution)/shard_map/ppermute | solution.py:26
  34.3 8.9 %collective-permute-start.5 = (f32[18,1,1024]{2,1,0:T(1,128)S(1)}, f32[18,1,1024]{2,1,0:T(1,128)S(1)}, u32[]{:S(2)}, u32[]{:S(2)}) collective-permute-start(f32[18,1,1024]{2,1,0:T(1,128)S(1)} %get-tuple-element.15), channel_id=1, source_target_pairs={{0,1},{1,2},{2,3},{3,4},{4,5},{5,6},{6,7},{7,8},{8,9},{9,10},{10,1... | collective-permute-start | bytes 221192 | tf_op jit(solution)/shard_map/ppermute | solution.py:23
  152.9 21.3 %copy-start = (f32[16,8,1024]{2,1,0:T(8,128)}, f32[16,8,1024]{2,1,0:T(8,128)S(1)}, u32[]{:S(2)}) copy-start(f32[16,8,1024]{2,1,0:T(8,128)S(1)} %multiply_add_fusion.4) | copy-start | bytes 1572868
  153.0 4.8 collective-permute-start.6
  155.8 5.2 collective-permute-start.7
  161.1 6.9 %collective-permute-start.8 = (f32[18,1,1024]{2,1,0:T(1,128)S(1)}, f32[18,1,1024]{2,1,0:T(1,128)S(1)}, u32[]{:S(2)}, u32[]{:S(2)}) collective-permute-start(f32[18,1,1024]{2,1,0:T(1,128)S(1)} %get-tuple-element.12), channel_id=1, source_target_pairs={{1,0},{2,1},{3,2},{4,3},{5,4},{6,5},{7,6},{8,7},{9,8},{10,9},{11,1... | collective-permute-start | bytes 221192 | tf_op jit(solution)/shard_map/ppermute | solution.py:26
  165.8 8.5 %copy-start.10 = (f32[16,8,1024]{2,1,0:T(8,128)S(1)}, f32[16,8,1024]{2,1,0:T(8,128)}, u32[]{:S(2)}) copy-start(f32[16,8,1024]{2,1,0:T(8,128)} %tile.63) | copy-start | bytes 1572868
  165.8 8.5 %copy-start.12 = (f32[16,8,1024]{2,1,0:T(8,128)S(1)}, f32[16,8,1024]{2,1,0:T(8,128)}, u32[]{:S(2)}) copy-start(f32[16,8,1024]{2,1,0:T(8,128)} %tile.67) | copy-start | bytes 1572868
  165.8 8.5 %collective-permute-start.9 = (f32[18,1,1024]{2,1,0:T(1,128)S(1)}, f32[18,1,1024]{2,1,0:T(1,128)S(1)}, u32[]{:S(2)}, u32[]{:S(2)}) collective-permute-start(f32[18,1,1024]{2,1,0:T(1,128)S(1)} %get-tuple-element.13), channel_id=1, source_target_pairs={{0,1},{1,2},{2,3},{3,4},{4,5},{5,6},{6,7},{7,8},{8,9},{9,10},{10,1... | collective-permute-start | bytes 221192 | tf_op jit(solution)/shard_map/ppermute | solution.py:23
  364.9 10.0 %collective-permute-start.10 = (f32[1,8,1024]{2,1,0:T(8,128)S(1)}, f32[1,8,1024]{2,1,0:T(8,128)S(1)}, u32[]{:S(2)}, u32[]{:S(2)}) collective-permute-start(f32[1,8,1024]{2,1,0:T(8,128)S(1)} %get-tuple-element.23), channel_id=1, source_target_pairs={{16,0},{32,16},{48,32},{64,48},{80,64},{96,80},{112,96},{128,112},... | collective-permute-start | bytes 98312 | tf_op jit(solution)/shard_map/ppermute | solution.py:26
  367.9 7.0 %collective-permute-start.11 = (f32[1,8,1024]{2,1,0:T(8,128)S(1)}, f32[1,8,1024]{2,1,0:T(8,128)S(1)}, u32[]{:S(2)}, u32[]{:S(2)}) collective-permute-start(f32[1,8,1024]{2,1,0:T(8,128)S(1)} %get-tuple-element.22), channel_id=1, source_target_pairs={{0,16},{16,32},{32,48},{48,64},{64,80},{80,96},{96,112},{112,128},... | collective-permute-start | bytes 98312 | tf_op jit(solution)/shard_map/ppermute | solution.py:23
  372.3 2.6 copy-start.2
  375.0 11.5 %collective-permute-start.12 = (f32[18,1,1024]{2,1,0:T(1,128)S(1)}, f32[18,1,1024]{2,1,0:T(1,128)S(1)}, u32[]{:S(2)}, u32[]{:S(2)}) collective-permute-start(f32[18,1,1024]{2,1,0:T(1,128)S(1)} %get-tuple-element.10), channel_id=1, source_target_pairs={{1,0},{2,1},{3,2},{4,3},{5,4},{6,5},{7,6},{8,7},{9,8},{10,9},{11,1... | collective-permute-start | bytes 221192 | tf_op jit(solution)/shard_map/ppermute | solution.py:26
  379.6 8.4 %collective-permute-start.13 = (f32[18,1,1024]{2,1,0:T(1,128)S(1)}, f32[18,1,1024]{2,1,0:T(1,128)S(1)}, u32[]{:S(2)}, u32[]{:S(2)}) collective-permute-start(f32[18,1,1024]{2,1,0:T(1,128)S(1)} %get-tuple-element.11), channel_id=1, source_target_pairs={{0,1},{1,2},{2,3},{3,4},{4,5},{5,6},{6,7},{7,8},{8,9},{9,10},{10,1... | collective-permute-start | bytes 221192 | tf_op jit(solution)/shard_map/ppermute | solution.py:23
  393.3 2.6 copy-start.4
  476.7 2.4 copy-start.17
  483.3 89.2 %copy-start.20 = (f32[128,16,64]{0,1,2:T(8,128)S(1)}, f32[128,16,64]{0,1,2:T(8,128)}, u32[]{:S(2)}) copy-start(f32[128,16,64]{0,1,2:T(8,128)} %copy.56) | copy-start | bytes 1572868
  586.3 20.5 %copy-start.9 = (f32[16,8,1024]{2,1,0:T(8,128)}, f32[16,8,1024]{2,1,0:T(8,128)S(1)}, u32[]{:S(2)}) copy-start(f32[16,8,1024]{2,1,0:T(8,128)S(1)} %add_add_fusion) | copy-start | bytes 1572868
  586.3 4.3 collective-permute-start.14
  588.3 5.2 collective-permute-start.15
  593.6 7.0 %collective-permute-start.16 = (f32[18,1,1024]{2,1,0:T(1,128)S(1)}, f32[18,1,1024]{2,1,0:T(1,128)S(1)}, u32[]{:S(2)}, u32[]{:S(2)}) collective-permute-start(f32[18,1,1024]{2,1,0:T(1,128)S(1)} %get-tuple-element.8), channel_id=1, source_target_pairs={{1,0},{2,1},{3,2},{4,3},{5,4},{6,5},{7,6},{8,7},{9,8},{10,9},{11,1... | collective-permute-start | bytes 221192 | tf_op jit(solution)/shard_map/ppermute | solution.py:26
  598.2 8.5 %copy-start.11 = (f32[16,8,1024]{2,1,0:T(8,128)S(1)}, f32[16,8,1024]{2,1,0:T(8,128)}, u32[]{:S(2)}) copy-start(f32[16,8,1024]{2,1,0:T(8,128)} %tile.63) | copy-start | bytes 1572868
  598.3 8.5 %copy-start.13 = (f32[16,8,1024]{2,1,0:T(8,128)S(1)}, f32[16,8,1024]{2,1,0:T(8,128)}, u32[]{:S(2)}) copy-start(f32[16,8,1024]{2,1,0:T(8,128)} %tile.67) | copy-start | bytes 1572868
  598.3 8.5 %copy-start.19 = (f32[16,8,1024]{2,1,0:T(8,128)S(1)}, f32[16,8,1024]{2,1,0:T(8,128)}, u32[]{:S(2)}) copy-start(f32[16,8,1024]{2,1,0:T(8,128)} %param.9) | copy-start | bytes 1572868
  598.3 8.5 %collective-permute-start.17 = (f32[18,1,1024]{2,1,0:T(1,128)S(1)}, f32[18,1,1024]{2,1,0:T(1,128)S(1)}, u32[]{:S(2)}, u32[]{:S(2)}) collective-permute-start(f32[18,1,1024]{2,1,0:T(1,128)S(1)} %get-tuple-element.9), channel_id=1, source_target_pairs={{0,1},{1,2},{2,3},{3,4},{4,5},{5,6},{6,7},{7,8},{8,9},{9,10},{10,1... | collective-permute-start | bytes 221192 | tf_op jit(solution)/shard_map/ppermute | solution.py:23
  (13 other events, 18.1 us)
where the time goes:
time: 617 us; the launch traced here: 609 us
  blocking collectives  373 us (60%)
  local copies, waits for them, and re-layouts  87.7 us (14%)
  starting transfers between devices  51.7 us (8%)
  other arithmetic  44.9 us (7%)
  matrix products  26 us (4%)
  waiting for transfers between devices  23.7 us (4%)
    psum x3, blocking collectives, total_gram(): return lax.psum(block_gram(former, latter, count_rhs), ('gx', 'gy'))  226 us
    psum x2, blocking collectives, body(): stacked = lax.psum(local_proj, ('gx', 'gy'))  146 us
    ppermute x8, starting transfers between devices, padded_2(): lax.ppermute(lax.slice_in_dim(block, 0, width, axis=dim), axis, backward)  29.8 us
    ppermute x8, waiting for transfers between devices, padded_2(): lax.ppermute(lax.slice_in_dim(block, block.shape[dim] - width, None, axis...  23.7 us
    ppermute x8, starting transfers between devices, padded_2(): lax.ppermute(lax.slice_in_dim(block, block.shape[dim] - width, None, axis...  16.3 us
    another operation x14, local copies, waits for them, and re-layouts, tiled(): return jnp.tile(values, (1, 1, count_rhs))  16.1 us
    dot_general x6, matrix products, block_gram(): return jnp.einsum('psz,ptz->st', left, right, precision=HIGH)  14 us
  transfers between devices with their start and end apart: 18, of which 6 were waited for; matrix products, arithmetic and copies ran while one was open for 5% of the time, Pallas kernels for 0%

commit v1 on v0

--- a/solution.py
+++ b/solution.py
@@ -133,7 +133,7 @@
     inv_piv = 1.0 / pivots
 
     def total_gram(former, latter):
-        return lax.psum(block_gram(former, latter, count_rhs), ("gx", "gy"))
+        return lax.psum(lax.psum(block_gram(former, latter, count_rhs), "gy"), "gx")
 
     start_res = right_side - apply_op(start_guess)
     first_factor, first_inv = chol_factor(total_gram(start_res, start_res))

time: 617 us -> 567 us (0.919)
  blocking collectives: 373 us -> 316 us
  starting transfers between devices: 51.7 us -> 59.1 us
    psum x3 -> x6, blocking collectives: 226 us -> 165 us  [total_gram(): return lax.psum(lax.psum(block_gram(former, latter, count_rhs), 'gy'), 'gx')]
    ppermute x8, starting transfers between devices: 29.8 us -> 36.6 us  [padded_2(): lax.ppermute(lax.slice_in_dim(block, 0, width, axis=dim), axis, backward)]
where the time goes in v1:
time: 567 us; the launch traced here: 558 us
  blocking collectives  316 us (56%)
  local copies, waits for them, and re-layouts  87.9 us (16%)
  starting transfers between devices  59.1 us (10%)
  other arithmetic  44.5 us (8%)
  matrix products  26 us (5%)
  waiting for transfers between devices  22.9 us (4%)
    psum x6, blocking collectives, total_gram(): return lax.psum(lax.psum(block_gram(former, latter, count_rhs), 'gy'), 'gx')  165 us
    psum x2, blocking collectives, body(): stacked = lax.psum(local_proj, ('gx', 'gy'))  150 us
    ppermute x8, starting transfers between devices, padded_2(): lax.ppermute(lax.slice_in_dim(block, 0, width, axis=dim), axis, backward)  36.6 us
    ppermute x8, waiting for transfers between devices, padded_2(): lax.ppermute(lax.slice_in_dim(block, block.shape[dim] - width, None, axis...  22.8 us
    ppermute x8, starting transfers between devices, padded_2(): lax.ppermute(lax.slice_in_dim(block, block.shape[dim] - width, None, axis...  16.9 us
    another operation x14, local copies, waits for them, and re-layouts, tiled(): return jnp.tile(values, (1, 1, count_rhs))  16.1 us
    dot_general x6, matrix products, block_gram(): return jnp.einsum('psz,ptz->st', left, right, precision=HIGH)  13.9 us
    reshape x5, local copies, waits for them, and re-layouts, block_gram(): left = former.reshape(cells, count_rhs, -1)  11.9 us
  transfers between devices with their start and end apart: 18, of which 6 were waited for; matrix products, arithmetic and copies ran while one was open for 5% of the time, Pallas kernels for 0%

profile of v1, /device:TPU:40, one launch (start us, length us, event | category | flops | bytes accessed | tf_op | source)
XLA Modules:
  0.0 558.1 jit_solution(18128831431237278926)
XLA Ops:
  3.4 3.6 collective-permute-start.2
  9.3 3.4 collective-permute-start.1
  29.8 4.6 collective-permute-start.4
  39.7 3.6 collective-permute-done.5
  43.3 3.8 fusion.36
  49.4 3.0 convolution_bitcast_fusion.12
  52.5 2.5 copy.35
  57.7 31.7 %psum.56 = f32[16,16]{0,1:T(8,128)S(1)} all-reduce(f32[16,16]{0,1:T(8,128)S(1)} %convolution_bitcast_fusion.12), channel_id=1, replica_groups=mesh['gx'=16,'gy'=16] {'gy'}, use_global_device_ids=true, to_apply=%region_0.1 | all-reduce | flops 256 | bytes 2048 | tf_op jit(solution)/shard_map/psum | solution.py:136
  89.4 23.2 %psum.57 = f32[16,16]{0,1:T(8,128)S(1)} all-reduce(f32[16,16]{0,1:T(8,128)S(1)} %psum.56), channel_id=1, replica_groups=mesh['gx'=16,'gy'=16] {'gx'}, use_global_device_ids=true, to_apply=%region_1.2 | all-reduce | flops 256 | bytes 2048 | tf_op jit(solution)/shard_map/psum | solution.py:136
  130.6 5.4 collective-permute-start.6
  137.9 3.3 collective-permute-done.7
  141.3 2.8 collective-permute-start.8
  144.2 3.2 collective-permute-start.9
  147.6 5.1 collective-permute-done.9
  160.9 75.1 %psum.58 = f32[16,16]{0,1:T(8,128)S(1)} all-reduce(f32[16,16]{0,1:T(8,128)S(1)} %convolution_bitcast_fusion.10), channel_id=1, replica_groups=mesh['gx'=16,'gy'=16] {'gx','gy'}, use_global_device_ids=true, to_apply=%region_4.7 | all-reduce | flops 256 | bytes 2048 | tf_op jit(solution)/shard_map/psum | solution.py:165
  250.1 3.0 convolution_bitcast_fusion.9
  253.2 33.9 %psum.59 = f32[16,16]{0,1:T(8,128)S(1)} all-reduce(f32[16,16]{0,1:T(8,128)S(1)} %convolution_bitcast_fusion.9), channel_id=1, replica_groups=mesh['gx'=16,'gy'=16] {'gy'}, use_global_device_ids=true, to_apply=%region_5.8 | all-reduce | flops 256 | bytes 2048 | tf_op jit(solution)/shard_map/psum | solution.py:136
  287.1 20.8 %psum.60 = f32[16,16]{0,1:T(8,128)S(1)} all-reduce(f32[16,16]{0,1:T(8,128)S(1)} %psum.59), channel_id=1, replica_groups=mesh['gx'=16,'gy'=16] {'gx'}, use_global_device_ids=true, to_apply=%region_6.9 | all-reduce | flops 256 | bytes 2048 | tf_op jit(solution)/shard_map/psum | solution.py:136
  327.6 5.0 collective-permute-start.10
  336.8 2.6 copy.56
  339.5 6.0 %collective-permute-start.12 = (f32[18,1,1024]{2,1,0:T(1,128)S(1)}, f32[18,1,1024]{2,1,0:T(1,128)S(1)}, u32[]{:S(2)}, u32[]{:S(2)}) collective-permute-start(f32[18,1,1024]{2,1,0:T(1,128)S(1)} %get-tuple-element.10), channel_id=1, source_target_pairs={{1,0},{2,1},{3,2},{4,3},{5,4},{6,5},{7,6},{8,7},{9,8},{10,9},{11,1... | collective-permute-start | bytes 221192 | tf_op jit(solution)/shard_map/ppermute | solution.py:26
  353.9 3.0 fusion.15
  359.1 2.6 copy.46
  364.5 75.3 %psum.61 = f32[2,16,16]{1,2,0:T(8,128)S(1)} all-reduce(f32[2,16,16]{1,2,0:T(8,128)S(1)} %pad_maximum_fusion.39), channel_id=1, replica_groups=mesh['gx'=16,'gy'=16] {'gx','gy'}, use_global_device_ids=true, to_apply=%region_7.10 | all-reduce | flops 512 | bytes 4096 | tf_op jit(solution)/shard_map/psum | solution.py:165
  449.5 3.1 convolution_bitcast_fusion.5
  452.6 33.9 %psum.62 = f32[16,16]{0,1:T(8,128)S(1)} all-reduce(f32[16,16]{0,1:T(8,128)S(1)} %convolution_bitcast_fusion.5), channel_id=1, replica_groups=mesh['gx'=16,'gy'=16] {'gy'}, use_global_device_ids=true, to_apply=%region_8.11 | all-reduce | flops 256 | bytes 2048 | tf_op jit(solution)/shard_map/psum | solution.py:136
  486.5 21.9 %psum.63 = f32[16,16]{0,1:T(8,128)S(1)} all-reduce(f32[16,16]{0,1:T(8,128)S(1)} %psum.62), channel_id=1, replica_groups=mesh['gx'=16,'gy'=16] {'gx'}, use_global_device_ids=true, to_apply=%region_9.12 | all-reduce | flops 256 | bytes 2048 | tf_op jit(solution)/shard_map/psum | solution.py:136
  512.3 2.9 cholesky.41
  533.2 4.8 collective-permute-start.14
  540.0 3.3 collective-permute-done.15
  543.4 4.4 collective-permute-start.16
  550.2 6.2 %collective-permute-done.17 = f32[18,1,1024]{2,1,0:T(1,128)S(1)} collective-permute-done((f32[18,1,1024]{2,1,0:T(1,128)S(1)}, f32[18,1,1024]{2,1,0:T(1,128)S(1)}, u32[]{:S(2)}, u32[]{:S(2)}) %collective-permute-start.17) | collective-permute-done | bytes 73760 | tf_op jit(solution)/shard_map/ppermute | solution.py:23
  (243 shorter events, 149.1 us)
Async XLA Ops:
  0.6 6.4 %copy-start.24 = (f32[16,8,64]{2,1,0:T(8,128)S(1)}, f32[16,8,64]{2,1,0:T(8,128)}, u32[]{:S(2)}) copy-start(f32[16,8,64]{2,1,0:T(8,128)} %param.11) | copy-start | bytes 98308
  0.6 8.6 %copy-start.23 = (f32[16,8,64]{2,1,0:T(8,128)S(1)}, f32[16,8,64]{2,1,0:T(8,128)}, u32[]{:S(2)}) copy-start(f32[16,8,64]{2,1,0:T(8,128)} %param.12) | copy-start | bytes 98308
  1.5 27.3 %collective-permute-start.3 = (f32[1,8,1024]{2,1,0:T(8,128)S(1)}, f32[1,8,1024]{2,1,0:T(8,128)S(1)}, u32[]{:S(2)}, u32[]{:S(2)}) collective-permute-start(f32[1,8,1024]{2,1,0:T(8,128)S(1)} %get-tuple-element.31), channel_id=1, source_target_pairs={{0,16},{16,32},{32,48},{48,64},{64,80},{80,96},{96,112},{112,128},... | collective-permute-start | bytes 98312 | tf_op jit(solution)/shard_map/ppermute | solution.py:23
  3.4 25.5 %collective-permute-start.2 = (f32[1,8,1024]{2,1,0:T(8,128)S(1)}, f32[1,8,1024]{2,1,0:T(8,128)S(1)}, u32[]{:S(2)}, u32[]{:S(2)}) collective-permute-start(f32[1,8,1024]{2,1,0:T(8,128)S(1)} %get-tuple-element.30), channel_id=1, source_target_pairs={{16,0},{32,16},{48,32},{64,48},{80,64},{96,80},{112,96},{128,112},... | collective-permute-start | bytes 98312 | tf_op jit(solution)/shard_map/ppermute | solution.py:26
  7.1 18.3 %collective-permute-start = (f32[1,8,64]{2,1,0:T(8,128)S(1)}, f32[1,8,64]{2,1,0:T(8,128)S(1)}, u32[]{:S(2)}, u32[]{:S(2)}) collective-permute-start(f32[1,8,64]{2,1,0:T(8,128)S(1)} %slice.369), channel_id=1, source_target_pairs={{0,16},{16,32},{32,48},{48,64},{64,80},{80,96},{96,112},{112,128},... | collective-permute-start | bytes 6152 | tf_op jit(solution)/shard_map/ppermute | solution.py:15
  9.3 27.0 %collective-permute-start.1 = (f32[16,1,64]{2,1,0:T(1,128)S(1)}, f32[16,1,64]{2,1,0:T(1,128)S(1)}, u32[]{:S(2)}, u32[]{:S(2)}) collective-permute-start(f32[16,1,64]{2,1,0:T(1,128)S(1)} %slice.371), channel_id=1, source_target_pairs={{0,1},{1,2},{2,3},{3,4},{4,5},{5,6},{6,7},{7,8},{8,9},{9,10},{10,1... | collective-permute-start | bytes 12296 | tf_op jit(solution)/shard_map/ppermute | solution.py:15
  26.4 2.4 copy-start.7
  29.8 9.9 %collective-permute-start.4 = (f32[18,1,1024]{2,1,0:T(1,128)S(1)}, f32[18,1,1024]{2,1,0:T(1,128)S(1)}, u32[]{:S(2)}, u32[]{:S(2)}) collective-permute-start(f32[18,1,1024]{2,1,0:T(1,128)S(1)} %get-tuple-element.14), channel_id=1, source_target_pairs={{1,0},{2,1},{3,2},{4,3},{5,4},{6,5},{7,6},{8,7},{9,8},{10,9},{11,1... | collective-permute-start | bytes 221192 | tf_op jit(solution)/shard_map/ppermute | solution.py:26
  34.3 8.9 %collective-permute-start.5 = (f32[18,1,1024]{2,1,0:T(1,128)S(1)}, f32[18,1,1024]{2,1,0:T(1,128)S(1)}, u32[]{:S(2)}, u32[]{:S(2)}) collective-permute-start(f32[18,1,1024]{2,1,0:T(1,128)S(1)} %get-tuple-element.15), channel_id=1, source_target_pairs={{0,1},{1,2},{2,3},{3,4},{4,5},{5,6},{6,7},{7,8},{8,9},{9,10},{10,1... | collective-permute-start | bytes 221192 | tf_op jit(solution)/shard_map/ppermute | solution.py:23
  130.6 22.1 %copy-start = (f32[16,8,1024]{2,1,0:T(8,128)}, f32[16,8,1024]{2,1,0:T(8,128)S(1)}, u32[]{:S(2)}) copy-start(f32[16,8,1024]{2,1,0:T(8,128)S(1)} %multiply_add_fusion.4) | copy-start | bytes 1572868
  130.6 7.3 %collective-permute-start.6 = (f32[1,8,1024]{2,1,0:T(8,128)S(1)}, f32[1,8,1024]{2,1,0:T(8,128)S(1)}, u32[]{:S(2)}, u32[]{:S(2)}) collective-permute-start(f32[1,8,1024]{2,1,0:T(8,128)S(1)} %get-tuple-element.27), channel_id=1, source_target_pairs={{16,0},{32,16},{48,32},{64,48},{80,64},{96,80},{112,96},{128,112},... | collective-permute-start | bytes 98312 | tf_op jit(solution)/shard_map/ppermute | solution.py:26
  136.0 5.2 collective-permute-start.7
  141.3 6.2 %collective-permute-start.8 = (f32[18,1,1024]{2,1,0:T(1,128)S(1)}, f32[18,1,1024]{2,1,0:T(1,128)S(1)}, u32[]{:S(2)}, u32[]{:S(2)}) collective-permute-start(f32[18,1,1024]{2,1,0:T(1,128)S(1)} %get-tuple-element.12), channel_id=1, source_target_pairs={{1,0},{2,1},{3,2},{4,3},{5,4},{6,5},{7,6},{8,7},{9,8},{10,9},{11,1... | collective-permute-start | bytes 221192 | tf_op jit(solution)/shard_map/ppermute | solution.py:26
  144.2 8.5 %copy-start.10 = (f32[16,8,1024]{2,1,0:T(8,128)S(1)}, f32[16,8,1024]{2,1,0:T(8,128)}, u32[]{:S(2)}) copy-start(f32[16,8,1024]{2,1,0:T(8,128)} %tile.63) | copy-start | bytes 1572868
  144.2 8.5 %copy-start.12 = (f32[16,8,1024]{2,1,0:T(8,128)S(1)}, f32[16,8,1024]{2,1,0:T(8,128)}, u32[]{:S(2)}) copy-start(f32[16,8,1024]{2,1,0:T(8,128)} %tile.67) | copy-start | bytes 1572868
  144.2 8.5 %collective-permute-start.9 = (f32[18,1,1024]{2,1,0:T(1,128)S(1)}, f32[18,1,1024]{2,1,0:T(1,128)S(1)}, u32[]{:S(2)}, u32[]{:S(2)}) collective-permute-start(f32[18,1,1024]{2,1,0:T(1,128)S(1)} %get-tuple-element.13), channel_id=1, source_target_pairs={{0,1},{1,2},{2,3},{3,4},{4,5},{5,6},{6,7},{7,8},{8,9},{9,10},{10,1... | collective-permute-start | bytes 221192 | tf_op jit(solution)/shard_map/ppermute | solution.py:23
  327.6 11.8 %collective-permute-start.10 = (f32[1,8,1024]{2,1,0:T(8,128)S(1)}, f32[1,8,1024]{2,1,0:T(8,128)S(1)}, u32[]{:S(2)}, u32[]{:S(2)}) collective-permute-start(f32[1,8,1024]{2,1,0:T(8,128)S(1)} %get-tuple-element.23), channel_id=1, source_target_pairs={{16,0},{32,16},{48,32},{64,48},{80,64},{96,80},{112,96},{128,112},... | collective-permute-start | bytes 98312 | tf_op jit(solution)/shard_map/ppermute | solution.py:26
  332.6 6.8 %collective-permute-start.11 = (f32[1,8,1024]{2,1,0:T(8,128)S(1)}, f32[1,8,1024]{2,1,0:T(8,128)S(1)}, u32[]{:S(2)}, u32[]{:S(2)}) collective-permute-start(f32[1,8,1024]{2,1,0:T(8,128)S(1)} %get-tuple-element.22), channel_id=1, source_target_pairs={{0,16},{16,32},{32,48},{48,64},{64,80},{80,96},{96,112},{112,128},... | collective-permute-start | bytes 98312 | tf_op jit(solution)/shard_map/ppermute | solution.py:23
  336.8 2.6 copy-start.2
  339.5 13.0 %collective-permute-start.12 = (f32[18,1,1024]{2,1,0:T(1,128)S(1)}, f32[18,1,1024]{2,1,0:T(1,128)S(1)}, u32[]{:S(2)}, u32[]{:S(2)}) collective-permute-start(f32[18,1,1024]{2,1,0:T(1,128)S(1)} %get-tuple-element.10), channel_id=1, source_target_pairs={{1,0},{2,1},{3,2},{4,3},{5,4},{6,5},{7,6},{8,7},{9,8},{10,9},{11,1... | collective-permute-start | bytes 221192 | tf_op jit(solution)/shard_map/ppermute | solution.py:26
  345.5 8.4 %collective-permute-start.13 = (f32[18,1,1024]{2,1,0:T(1,128)S(1)}, f32[18,1,1024]{2,1,0:T(1,128)S(1)}, u32[]{:S(2)}, u32[]{:S(2)}) collective-permute-start(f32[18,1,1024]{2,1,0:T(1,128)S(1)} %get-tuple-element.11), channel_id=1, source_target_pairs={{0,1},{1,2},{2,3},{3,4},{4,5},{5,6},{6,7},{7,8},{8,9},{9,10},{10,1... | collective-permute-start | bytes 221192 | tf_op jit(solution)/shard_map/ppermute | solution.py:23
  359.1 2.6 copy-start.4
  449.5 69.9 %copy-start.20 = (f32[128,16,64]{0,1,2:T(8,128)S(1)}, f32[128,16,64]{0,1,2:T(8,128)}, u32[]{:S(2)}) copy-start(f32[128,16,64]{0,1,2:T(8,128)} %copy.56) | copy-start | bytes 1572868
  523.2 2.4 copy-start.21
  533.2 23.2 %copy-start.9 = (f32[16,8,1024]{2,1,0:T(8,128)}, f32[16,8,1024]{2,1,0:T(8,128)S(1)}, u32[]{:S(2)}) copy-start(f32[16,8,1024]{2,1,0:T(8,128)S(1)} %add_add_fusion) | copy-start | bytes 1572868
  533.2 6.8 %collective-permute-start.14 = (f32[1,8,1024]{2,1,0:T(8,128)S(1)}, f32[1,8,1024]{2,1,0:T(8,128)S(1)}, u32[]{:S(2)}, u32[]{:S(2)}) collective-permute-start(f32[1,8,1024]{2,1,0:T(8,128)S(1)} %get-tuple-element.19), channel_id=1, source_target_pairs={{16,0},{32,16},{48,32},{64,48},{80,64},{96,80},{112,96},{128,112},... | collective-permute-start | bytes 98312 | tf_op jit(solution)/shard_map/ppermute | solution.py:26
  538.1 5.2 collective-permute-start.15
  543.4 6.7 %collective-permute-start.16 = (f32[18,1,1024]{2,1,0:T(1,128)S(1)}, f32[18,1,1024]{2,1,0:T(1,128)S(1)}, u32[]{:S(2)}, u32[]{:S(2)}) collective-permute-start(f32[18,1,1024]{2,1,0:T(1,128)S(1)} %get-tuple-element.8), channel_id=1, source_target_pairs={{1,0},{2,1},{3,2},{4,3},{5,4},{6,5},{7,6},{8,7},{9,8},{10,9},{11,1... | collective-permute-start | bytes 221192 | tf_op jit(solution)/shard_map/ppermute | solution.py:26
  547.9 8.5 %copy-start.11 = (f32[16,8,1024]{2,1,0:T(8,128)S(1)}, f32[16,8,1024]{2,1,0:T(8,128)}, u32[]{:S(2)}) copy-start(f32[16,8,1024]{2,1,0:T(8,128)} %tile.63) | copy-start | bytes 1572868
  547.9 8.5 %copy-start.13 = (f32[16,8,1024]{2,1,0:T(8,128)S(1)}, f32[16,8,1024]{2,1,0:T(8,128)}, u32[]{:S(2)}) copy-start(f32[16,8,1024]{2,1,0:T(8,128)} %tile.67) | copy-start | bytes 1572868
  547.9 8.5 %copy-start.19 = (f32[16,8,1024]{2,1,0:T(8,128)S(1)}, f32[16,8,1024]{2,1,0:T(8,128)}, u32[]{:S(2)}) copy-start(f32[16,8,1024]{2,1,0:T(8,128)} %param.9) | copy-start | bytes 1572868
  547.9 8.5 %collective-permute-start.17 = (f32[18,1,1024]{2,1,0:T(1,128)S(1)}, f32[18,1,1024]{2,1,0:T(1,128)S(1)}, u32[]{:S(2)}, u32[]{:S(2)}) collective-permute-start(f32[18,1,1024]{2,1,0:T(1,128)S(1)} %get-tuple-element.9), channel_id=1, source_target_pairs={{0,1},{1,2},{2,3},{3,4},{4,5},{5,6},{6,7},{7,8},{8,9},{9,10},{10,1... | collective-permute-start | bytes 221192 | tf_op jit(solution)/shard_map/ppermute | solution.py:23
  (13 other events, 18.1 us)
